TPU v7x, 32 devices: a whole 2x2x4 slice. The times are simulated.
32 devices in a mesh: row: 8 (over y, x, core), col: 4 (over z).
Axes of the slice: x: 2, y: 2, z: 4, core: 2. Of those that a mesh axis runs over, the one named last changes fastest.
Arguments:
- adjacency: float32 [1024, 32768], P('row', 'col'), may hold values from 0 to 0.99, as said below
Outputs:
- tom: float32 [1024, 1024], P('row', 'col')
Inputs may be any that keep to these rules, and one draw needn't show every extreme that they name: `adjacency`: every entry is nonnegative and below 0.99.
All inputs are finite; a program needn't handle non-finite values.
Results may differ from a plain program's by a relative error of at most 0.000059.
Values sent between devices are 32-bit elements; how exact they have to be, the bound alone decides.
No kernel may reach another device: no remote copies, remote signals or barrier semaphores. Data moves between devices by JAX's collectives and lax.ppermute only.
A program may use at most 64 MiB of HBM per device.

v0:
```python
import jax
import jax.numpy as jnp
from jax import lax
from jax.sharding import PartitionSpec as P


def inner_rows(left, right):
    return lax.dot_general(
        left,
        right,
        (((1,), (1,)), ((), ())),
        precision=lax.Precision.HIGHEST,
        preferred_element_type=jnp.float32,
    )


def body(adjacency):
    strip_rows = adjacency.shape[0]
    window = strip_rows * lax.axis_size("row") // lax.axis_size("col")
    pieces = lax.all_to_all(adjacency, "row", split_axis=1, concat_axis=0, tiled=True)
    block_sums = lax.psum_scatter(
        inner_rows(pieces, pieces), "col", scatter_dimension=0, tiled=True
    )
    shared_sum = lax.psum_scatter(block_sums, "row", scatter_dimension=1, tiled=True).T
    own_degree = lax.psum(jnp.sum(adjacency, axis=1), "col")
    all_degree = lax.all_gather(own_degree, "row", axis=0, tiled=True)
    col_degree = lax.dynamic_slice_in_dim(all_degree, lax.axis_index("col") * window, window, 0)
    linked = adjacency[:, :window]
    smaller = jnp.minimum(own_degree[:, None], col_degree[None, :])
    return (shared_sum + linked) / (smaller + 1.0 - linked)


def solution(mesh):
    placed = (P("row", "col"),)
    return jax.shard_map(
        body, mesh=mesh, in_specs=placed, out_specs=P("row", "col"), check_vma=False
    )
```

profile of v0, /device:TPU:0, one launch (start us, length us, event | category | flops | bytes accessed | tf_op | source)
XLA Modules:
  0.0 215.7 jit_solution(15998971876274687652)
XLA Ops:
  6.5 0.0 reduce-scatter.3.cloned.1.call-start
  6.5 5.6 %copy.10 = f32[128,8192]{0,1:T(8,128)} copy(f32[128,8192]{1,0:T(8,128)} %param.1) | data formatting | bytes 8388608 | tf_op args[0]
  12.1 54.3 %all_to_all.19 = f32[128,8,1024]{0,2,1:T(8,128)} all-to-all(f32[128,8,1024]{0,2,1:T(8,128)} %bitcast.11), channel_id=1, replica_groups=mesh['row'=8,'col'=4] {'row'}, dimensions={1} | all-to-all | bytes 8388608 | tf_op jit(solution)/shard_map/all_to_all | solution.py:20
  66.4 5.3 %copy.11 = f32[8,128,1024]{2,1,0:T(8,128)} copy(f32[8,128,1024]{1,2,0:T(8,128)} %bitcast.12) | data formatting | bytes 8388608 | tf_op jit(solution)/shard_map/all_to_all | solution.py:20
  71.8 18.1 %fusion.1 = f32[1024,1024]{1,0:T(8,128)} fusion(f32[1024,1024]{1,0:T(8,128)} %bitcast.13), kind=kOutput, calls=%fused_computation.2 | convolution fusion | flops 12884901888 | bytes 8388608 | tf_op jit(solution)/shard_map/dot_general | solution.py:8
  89.9 0.0 reduce-scatter.3.cloned.1.call-update
  89.9 0.0 reduce-scatter.5.cloned.1.call-start
  90.0 76.9 %reduce-scatter.3.cloned.1.call-done = f32[256,1024]{1,0:T(8,128)} async-done(((f32[1024,1024]{1,0:T(8,128)}), f32[256,1024]{1,0:T(8,128)}) %reduce-scatter.3.cloned.1.call-update) | async-done | bytes 1048592 | tf_op jit(solution)/shard_map/reduce_scatter | solution.py:21
  166.9 0.0 reduce-scatter.5.cloned.1.call-update
  166.9 2.5 %reduce_sum.9 = f32[128]{0:T(128)S(1)} reduce(f32[128,8192]{1,0:T(8,128)} %param.1, f32[]{:T(128)} %constant.6.clone.1), dimensions={1}, to_apply=%region_2.0 | reduce | flops 1048448 | bytes 4194820 | tf_op jit(solution)/shard_map/reduce_sum | solution.py:25
  169.4 11.0 %psum.7 = f32[128]{0:T(128)S(1)} all-reduce(f32[128]{0:T(128)S(1)} %reduce_sum.9), channel_id=1, replica_groups=mesh['row'=8,'col'=4] {'col'}, use_global_device_ids=true, to_apply=%region_3.0 | all-reduce | flops 128 | bytes 1024 | tf_op jit(solution)/shard_map/psum | solution.py:25
  180.4 8.9 %all-gather = f32[8,1,128]{2,1,0:T(1,128)S(1)} all-gather(f32[1,1,128]{2,1,0:T(1,128)S(1)} %bitcast.15), channel_id=1, replica_groups=mesh['row'=8,'col'=4] {'row'}, dimensions={0}, use_global_device_ids=true | all-gather | bytes 4608 | tf_op jit(solution)/shard_map/all_gather | solution.py:26
  189.3 0.1 dynamic_slice.3
  189.4 17.6 %reduce-scatter.5.cloned.1.call-done = f32[256,128]{1,0:T(8,128)} async-done(((f32[256,1024]{1,0:T(8,128)}), f32[256,128]{1,0:T(8,128)}) %reduce-scatter.5.cloned.1.call-update) | async-done | bytes 131088 | tf_op jit(solution)/shard_map/reduce_scatter | solution.py:24
  207.0 1.1 fusion
  208.1 0.8 copy.13
Async XLA Ops:
  6.5 160.4 %reduce-scatter.3.cloned.1.call-start = ((), (), s32[]{:S(2)}) async-start(), calls=%async_computation.3 | async-start | bytes 5242880 | tf_op jit(solution)/shard_map/reduce_scatter | solution.py:21
  89.9 117.1 %reduce-scatter.5.cloned.1.call-start = ((), (), s32[]{:S(2)}) async-start(), calls=%async_computation.4 | async-start | bytes 1179648 | tf_op jit(solution)/shard_map/reduce_scatter | solution.py:24
Sparse Core Ops, SparseCore 0:
  90.1 76.8 reduce-scatter.2
  170.4 36.5 reduce-scatter.4
where the time goes:
time: 216 us
  waiting for transfers between devices  94.6 us (44%)
  blocking collectives  74.2 us (34%)
  matrix products  18.1 us (8%)
  between operations  13.4 us (6%)
  local copies, waits for them, and re-layouts  11.7 us (5%)
  other arithmetic  3.57 us (2%)
    reduce_scatter x1, waiting for transfers between devices, body(): lax.psum_scatter(inner_rows(pieces, pieces), 'col', scatter_dimension=0,...  76.9 us
    all_to_all x1, blocking collectives, body(): lax.all_to_all(adjacency, 'row', split_axis=1, concat_axis=0, tiled=True)  54.3 us
    dot_general x1, matrix products, inner_rows(): lax.dot_general(left, right, (((1,), (1,)), ((), ())), precision=lax.Prec...  18.1 us
    reduce_scatter x1, waiting for transfers between devices, body(): lax.psum_scatter(block_sums, 'row', scatter_dimension=1, tiled=True)  17.6 us
    psum x1, blocking collectives, body(): own_degree = lax.psum(jnp.sum(adjacency, axis=1), 'col')  11 us
    all_gather x1, blocking collectives, body(): all_degree = lax.all_gather(own_degree, 'row', axis=0, tiled=True)  8.92 us
    unnamed x1, local copies, waits for them, and re-layouts  5.57 us
    all_to_all x1, local copies, waits for them, and re-layouts, body(): lax.all_to_all(adjacency, 'row', split_axis=1, concat_axis=0, tiled=True)  5.34 us
  transfers between devices with their start and end apart: 2, of which 2 were waited for; matrix products, arithmetic and copies ran while one was open for 1% of the time, Pallas kernels for 0%

commit v1 on v0

--- a/solution.py
+++ b/solution.py
@@ -23,7 +23,12 @@
     )
     shared_sum = lax.psum_scatter(block_sums, "row", scatter_dimension=1, tiled=True).T
     own_degree = lax.psum(jnp.sum(adjacency, axis=1), "col")
-    all_degree = lax.all_gather(own_degree, "row", axis=0, tiled=True)
+    ring = [own_degree]
+    for hop in range(7):
+        ring.append(lax.ppermute(ring[-1], "row", [(dev, (dev + 1) % 8) for dev in range(8)]))
+    all_degree = jnp.roll(
+        jnp.concatenate(ring[::-1], axis=0), (lax.axis_index("row") + 1) * ring[0].shape[0], axis=0
+    )
     col_degree = lax.dynamic_slice_in_dim(all_degree, lax.axis_index("col") * window, window, 0)
     linked = adjacency[:, :window]
     smaller = jnp.minimum(own_degree[:, None], col_degree[None, :])

time: 216 us -> 216 us (level)
  blocking collectives: 74.2 us -> 67.3 us
  waiting for transfers between devices: 94.6 us -> 101 us
    reduce_scatter x1, waiting for transfers between devices: 76.9 us -> 34.6 us  [body(): lax.psum_scatter(inner_rows(pieces, pieces), 'col', scatter_dimension=0,...]
    ppermute x0 -> x7, waiting for transfers between devices: none -> 27 us  [body(): lax.ppermute(ring[-1], 'row', [(dev, (dev + 1) % 8) for dev in range(8)])]
    reduce_scatter x1, waiting for transfers between devices: 17.6 us -> 39.6 us  [body(): lax.psum_scatter(block_sums, 'row', scatter_dimension=1, tiled=True)]
    all_gather x1 -> x0, blocking collectives: 8.92 us -> none  [body(): all_degree = lax.all_gather(own_degree, 'row', axis=0, tiled=True)]
    unnamed x1 -> x16, local copies, waits for them, and re-layouts: 5.57 us -> 5.66 us
  transfers between devices with their start and end apart: 2 -> 9, of which waited for: 2 -> 9; matrix products, arithmetic and copies ran while one was open for 1% -> 1% of each run, Pallas kernels for 0% -> 0%
where the time goes in v1:
time: 216 us
  waiting for transfers between devices  101 us (47%)
  blocking collectives  67.3 us (31%)
  matrix products  18.1 us (8%)
  between operations  13.5 us (6%)
  local copies, waits for them, and re-layouts  11.9 us (6%)
  other arithmetic  3.57 us (2%)
    all_to_all x1, blocking collectives, body(): lax.all_to_all(adjacency, 'row', split_axis=1, concat_axis=0, tiled=True)  54.3 us
    reduce_scatter x1, waiting for transfers between devices, body(): lax.psum_scatter(block_sums, 'row', scatter_dimension=1, tiled=True)  39.6 us
    reduce_scatter x1, waiting for transfers between devices, body(): lax.psum_scatter(inner_rows(pieces, pieces), 'col', scatter_dimension=0,...  34.6 us
    ppermute x7, waiting for transfers between devices, body(): lax.ppermute(ring[-1], 'row', [(dev, (dev + 1) % 8) for dev in range(8)])  27 us
    dot_general x1, matrix products, inner_rows(): lax.dot_general(left, right, (((1,), (1,)), ((), ())), precision=lax.Prec...  18.1 us
    psum x1, blocking collectives, body(): own_degree = lax.psum(jnp.sum(adjacency, axis=1), 'col')  13 us
    unnamed x16, local copies, waits for them, and re-layouts  5.66 us
    all_to_all x1, local copies, waits for them, and re-layouts, body(): lax.all_to_all(adjacency, 'row', split_axis=1, concat_axis=0, tiled=True)  5.35 us
  transfers between devices with their start and end apart: 9, of which 9 were waited for; matrix products, arithmetic and copies ran while one was open for 1% of the time, Pallas kernels for 0%

profile of v1, /device:TPU:0, one launch (start us, length us, event | category | flops | bytes accessed | tf_op | source)
XLA Modules:
  0.0 215.8 jit_solution(13704399934065595680)
XLA Ops:
  6.5 5.6 %copy.6 = f32[128,8192]{0,1:T(8,128)} copy(f32[128,8192]{1,0:T(8,128)} %param.1) | data formatting | bytes 8388608 | tf_op args[0]
  12.1 54.3 %all_to_all.19 = f32[128,8,1024]{0,2,1:T(8,128)} all-to-all(f32[128,8,1024]{0,2,1:T(8,128)} %bitcast.9), channel_id=1, replica_groups=mesh['row'=8,'col'=4] {'row'}, dimensions={1} | all-to-all | bytes 8388608 | tf_op jit(solution)/shard_map/all_to_all | solution.py:20
  66.4 5.4 %copy.7 = f32[8,128,1024]{2,1,0:T(8,128)} copy(f32[8,128,1024]{1,2,0:T(8,128)} %bitcast.10) | data formatting | bytes 8388608 | tf_op jit(solution)/shard_map/all_to_all | solution.py:20
  71.8 18.1 %fusion.1 = f32[1024,1024]{1,0:T(8,128)} fusion(f32[1024,1024]{1,0:T(8,128)} %bitcast.11), kind=kOutput, calls=%fused_computation.18 | convolution fusion | flops 12884901888 | bytes 8388608 | tf_op jit(solution)/shard_map/dot_general | solution.py:8
  89.9 0.0 reduce-scatter.3.cloned.1.call-update
  90.0 0.0 reduce-scatter.5.cloned.1.call-start
  90.0 2.5 %reduce_sum.9 = f32[128]{0:T(128)S(1)} reduce(f32[128,8192]{1,0:T(8,128)} %param.1, f32[]{:T(128)} %constant.35.clone.1), dimensions={1}, to_apply=%region_2.0 | reduce | flops 1048448 | bytes 4194820 | tf_op jit(solution)/shard_map/reduce_sum | solution.py:25
  92.5 13.0 %psum.7 = f32[128]{0:T(128)S(1)} all-reduce(f32[128]{0:T(128)S(1)} %reduce_sum.9), channel_id=1, replica_groups=mesh['row'=8,'col'=4] {'col'}, use_global_device_ids=true, to_apply=%region_3.0 | all-reduce | flops 128 | bytes 1024 | tf_op jit(solution)/shard_map/psum | solution.py:25
  105.5 0.0 collective-permute-start
  105.6 3.9 %collective-permute-done = f32[128]{0:T(128)S(1)} collective-permute-done((f32[128]{0:T(128)S(1)}, f32[128]{0:T(128)S(1)}, u32[]{:S(2)}, u32[]{:S(2)}) %collective-permute-start) | collective-permute-done | bytes 544 | tf_op jit(solution)/shard_map/ppermute | solution.py:28
  109.4 3.9 %collective-permute-done.1 = f32[128]{0:T(128)S(1)} collective-permute-done((f32[128]{0:T(128)S(1)}, f32[128]{0:T(128)S(1)}, u32[]{:S(2)}, u32[]{:S(2)}) %collective-permute-start.1) | collective-permute-done | bytes 544 | tf_op jit(solution)/shard_map/ppermute | solution.py:28
  113.3 0.0 collective-permute-start.2
  113.3 3.9 %collective-permute-done.2 = f32[128]{0:T(128)S(1)} collective-permute-done((f32[128]{0:T(128)S(1)}, f32[128]{0:T(128)S(1)}, u32[]{:S(2)}, u32[]{:S(2)}) %collective-permute-start.2) | collective-permute-done | bytes 544 | tf_op jit(solution)/shard_map/ppermute | solution.py:28
  117.1 0.0 collective-permute-start.3
  117.1 3.9 %collective-permute-done.3 = f32[128]{0:T(128)S(1)} collective-permute-done((f32[128]{0:T(128)S(1)}, f32[128]{0:T(128)S(1)}, u32[]{:S(2)}, u32[]{:S(2)}) %collective-permute-start.3) | collective-permute-done | bytes 544 | tf_op jit(solution)/shard_map/ppermute | solution.py:28
  121.0 3.9 %collective-permute-done.4 = f32[128]{0:T(128)S(1)} collective-permute-done((f32[128]{0:T(128)S(1)}, f32[128]{0:T(128)S(1)}, u32[]{:S(2)}, u32[]{:S(2)}) %collective-permute-start.4) | collective-permute-done | bytes 544 | tf_op jit(solution)/shard_map/ppermute | solution.py:28
  124.9 3.9 %collective-permute-done.5 = f32[128]{0:T(128)S(1)} collective-permute-done((f32[128]{0:T(128)S(1)}, f32[128]{0:T(128)S(1)}, u32[]{:S(2)}, u32[]{:S(2)}) %collective-permute-start.5) | collective-permute-done | bytes 544 | tf_op jit(solution)/shard_map/ppermute | solution.py:28
  128.7 3.9 %collective-permute-done.6 = f32[128]{0:T(128)S(1)} collective-permute-done((f32[128]{0:T(128)S(1)}, f32[128]{0:T(128)S(1)}, u32[]{:S(2)}, u32[]{:S(2)}) %collective-permute-start.6) | collective-permute-done | bytes 544 | tf_op jit(solution)/shard_map/ppermute | solution.py:28
  132.6 34.6 %reduce-scatter.3.cloned.1.call-done = f32[256,1024]{1,0:T(8,128)} async-done(((f32[1024,1024]{1,0:T(8,128)}), f32[256,1024]{1,0:T(8,128)}) %reduce-scatter.3.cloned.1.call-update) | async-done | bytes 1048592 | tf_op jit(solution)/shard_map/reduce_scatter | solution.py:21
  167.2 0.0 reduce-scatter.5.cloned.1.call-update
  167.4 0.1 dynamic_slice.8
  167.5 39.6 %reduce-scatter.5.cloned.1.call-done = f32[256,128]{1,0:T(8,128)} async-done(((f32[256,1024]{1,0:T(8,128)}), f32[256,128]{1,0:T(8,128)}) %reduce-scatter.5.cloned.1.call-update) | async-done | bytes 131088 | tf_op jit(solution)/shard_map/reduce_scatter | solution.py:24
  207.1 1.1 fusion
  208.2 0.8 copy.9
  (22 shorter events, 0.1 us)
Async XLA Ops:
  6.5 160.6 %reduce-scatter.3.cloned.1.call-start = ((), (), s32[]{:S(2)}) async-start(), calls=%async_computation.3 | async-start | bytes 5242880 | tf_op jit(solution)/shard_map/reduce_scatter | solution.py:21
  90.0 117.2 %reduce-scatter.5.cloned.1.call-start = ((), (), s32[]{:S(2)}) async-start(), calls=%async_computation.4 | async-start | bytes 1179648 | tf_op jit(solution)/shard_map/reduce_scatter | solution.py:24
  105.5 3.9 %collective-permute-start = (f32[128]{0:T(128)S(1)}, f32[128]{0:T(128)S(1)}, u32[]{:S(2)}, u32[]{:S(2)}) collective-permute-start(f32[128]{0:T(128)S(1)} %psum.7), channel_id=1, source_target_pairs={{0,4},{4,8},{8,12},{12,16},{16,20},{20,24},{24,28},{28,0},{1,5},{5... | collective-permute-start | bytes 1544 | tf_op jit(solution)/shard_map/ppermute | solution.py:28
  109.4 3.9 %collective-permute-start.1 = (f32[128]{0:T(128)S(1)}, f32[128]{0:T(128)S(1)}, u32[]{:S(2)}, u32[]{:S(2)}) collective-permute-start(f32[128]{0:T(128)S(1)} %collective-permute-done), channel_id=1, source_target_pairs={{0,4},{4,8},{8,12},{12,16},{16,20},{20,24},{24,28},{28,0},{1,5},{5... | collective-permute-start | bytes 1544 | tf_op jit(solution)/shard_map/ppermute | solution.py:28
  113.3 3.9 %collective-permute-start.2 = (f32[128]{0:T(128)S(1)}, f32[128]{0:T(128)S(1)}, u32[]{:S(2)}, u32[]{:S(2)}) collective-permute-start(f32[128]{0:T(128)S(1)} %collective-permute-done.1), channel_id=1, source_target_pairs={{0,4},{4,8},{8,12},{12,16},{16,20},{20,24},{24,28},{28,0},{1,5},{5... | collective-permute-start | bytes 1544 | tf_op jit(solution)/shard_map/ppermute | solution.py:28
  117.1 3.9 %collective-permute-start.3 = (f32[128]{0:T(128)S(1)}, f32[128]{0:T(128)S(1)}, u32[]{:S(2)}, u32[]{:S(2)}) collective-permute-start(f32[128]{0:T(128)S(1)} %collective-permute-done.2), channel_id=1, source_target_pairs={{0,4},{4,8},{8,12},{12,16},{16,20},{20,24},{24,28},{28,0},{1,5},{5... | collective-permute-start | bytes 1544 | tf_op jit(solution)/shard_map/ppermute | solution.py:28
  121.0 3.9 %collective-permute-start.4 = (f32[128]{0:T(128)S(1)}, f32[128]{0:T(128)S(1)}, u32[]{:S(2)}, u32[]{:S(2)}) collective-permute-start(f32[128]{0:T(128)S(1)} %collective-permute-done.3), channel_id=1, source_target_pairs={{0,4},{4,8},{8,12},{12,16},{16,20},{20,24},{24,28},{28,0},{1,5},{5... | collective-permute-start | bytes 1544 | tf_op jit(solution)/shard_map/ppermute | solution.py:28
  124.9 3.9 %collective-permute-start.5 = (f32[128]{0:T(128)S(1)}, f32[128]{0:T(128)S(1)}, u32[]{:S(2)}, u32[]{:S(2)}) collective-permute-start(f32[128]{0:T(128)S(1)} %collective-permute-done.4), channel_id=1, source_target_pairs={{0,4},{4,8},{8,12},{12,16},{16,20},{20,24},{24,28},{28,0},{1,5},{5... | collective-permute-start | bytes 1544 | tf_op jit(solution)/shard_map/ppermute | solution.py:28
  128.7 3.9 %collective-permute-start.6 = (f32[128]{0:T(128)S(1)}, f32[128]{0:T(128)S(1)}, u32[]{:S(2)}, u32[]{:S(2)}) collective-permute-start(f32[128]{0:T(128)S(1)} %collective-permute-done.5), channel_id=1, source_target_pairs={{0,4},{4,8},{8,12},{12,16},{16,20},{20,24},{24,28},{28,0},{1,5},{5... | collective-permute-start | bytes 1544 | tf_op jit(solution)/shard_map/ppermute | solution.py:28
Sparse Core Ops, SparseCore 0:
  90.1 77.0 reduce-scatter.2
  170.7 36.4 reduce-scatter.4
